TPU v7x, 512 devices: a whole 4x8x8 slice. The times are simulated.
512 devices in a mesh: ctx: 16 (over y, x_hi), tp: 32 (over z, x_lo, core).
Axes of the slice: x: 4 (x_hi: 2, x_lo: 2; x = x_hi * 2 + x_lo), y: 8, z: 8, core: 2. Of those that a mesh axis runs over, the one named last changes fastest.
Arguments:
- resid_in: bfloat16 [2048, 4096], P('ctx', 'tp'), may hold values from -6 to 6
- feats: bfloat16 [2048, 3, 4096], P('ctx', None, 'tp'), may hold values from -6 to 6
- short_filter: float32 [3, 3, 4096], P(None, None, 'tp'), may hold values from -3.5 to 3.5
- residues: float32 [4096, 16], P('tp'), may hold values from -4 to 4
- rates: float32 [4096, 16], P('tp'), may hold values from 0.00014648438 to 0.03
- out_weight: bfloat16 [4096, 4096], P('tp'), may hold values from -0.1875 to 0.1875
- norm_gain: float32 [4096], replicated, may hold values from 0.1 to 1.9
- attn_weight: bfloat16 [4096, 3, 4096], P(None, None, 'tp'), may hold values from -1 to 1
Outputs:
- hyena_out: bfloat16 [2048, 4096], P('ctx', 'tp')
- context: bfloat16 [2048, 4096], P('ctx', 'tp')
All inputs are finite; a program needn't handle non-finite values.
Results may differ from a plain program's by a relative error of at most 0.01.
Values may be sent and summed in bfloat16 or wider, within the bound.
No kernel may reach another device: no remote copies, remote signals or barrier semaphores. Data moves between devices by JAX's collectives and lax.ppermute only.
A program may use at most 192 MiB of HBM per device.

v0:
```python
import math
import jax
import jax.numpy as jnp
from jax import lax
from jax.sharding import PartitionSpec as P

HEAD_DIM = 128
eps_norm = 1e-05
rope_base = 10000.0
mask_fill = -1e30
highest = lax.Precision.HIGHEST


def shifted(value, axis, steps):
    count = lax.axis_size(axis)
    initial, last = (max(0, -steps), min(count, count - steps))
    return lax.ppermute(value, axis, [(source, source + steps) for source in range(initial, last)])


def toeplitz_lower(filter_taps):
    chan_count, block_size = filter_taps.shape
    padded = jnp.concatenate(
        [jnp.zeros((chan_count, block_size - 1), jnp.float32), filter_taps], axis=1
    )
    flipped = padded[:, ::-1]
    tiled = jnp.tile(flipped, (1, block_size))
    offset = block_size - 1
    window = tiled[:, offset : offset + block_size * (2 * block_size - 2)]
    return window.reshape(chan_count, block_size, 2 * block_size - 2)[:, :, :block_size]


def modal_conv(signal, residues, rates, start_state):
    chan_count, length = signal.shape
    block_size = math.gcd(length, 128)
    block_count = length // block_size
    weight = residues * jnp.sqrt(1.0 - jnp.exp(-2.0 * rates))
    lag_steps = jnp.arange(block_size, dtype=jnp.float32)
    powers = jnp.exp(-rates[:, :, None] * lag_steps)
    filter_taps = jnp.sum(weight[:, :, None] * powers, axis=1)
    toeplitz = toeplitz_lower(filter_taps)
    blocks = signal.reshape(chan_count, block_count, block_size)
    inner_part = jnp.einsum("cij,cnj->cni", toeplitz, blocks, precision=highest)
    tail_powers = jnp.exp(-rates[:, :, None] * (block_size - lag_steps))
    end_states = jnp.einsum("cnj,cmj->cnm", blocks, tail_powers, precision=highest)
    block_steps = jnp.arange(block_count, dtype=jnp.float32)
    gap_count = block_steps[:, None] - 1.0 - block_steps[None, :]
    live_mask = gap_count >= 0.0
    carry_mat = jnp.where(
        live_mask, jnp.exp(-rates[:, :, None, None] * block_size * jnp.maximum(gap_count, 0.0)), 0.0
    )
    states = jnp.einsum("cmnk,ckm->cnm", carry_mat, end_states, precision=highest)
    states = (
        states
        + jnp.exp(-rates[:, None, :] * block_size * block_steps[None, :, None])
        * start_state[:, None, :]
    )
    cross_part = jnp.einsum("cnm,cmi->cni", states * weight[:, None, :], powers, precision=highest)
    return (inner_part + cross_part).reshape(chan_count, length)


def short_mix(feats, short_filter):
    row_count = feats.shape[0]
    prior_feats = shifted(feats[-2:], "ctx", 1)
    joined = jnp.concatenate([prior_feats, feats], axis=0).astype(jnp.float32)
    return (
        short_filter[0] * joined[2:]
        + short_filter[1] * joined[1 : row_count + 1]
        + short_filter[2] * joined[:row_count]
    )


def rotary_turn(vectors, positions):
    half_dim = vectors.shape[-1] // 2
    frequency = rope_base ** (-jnp.arange(half_dim, dtype=jnp.float32) * 2.0 / vectors.shape[-1])
    angles = positions.astype(jnp.float32)[:, None] * frequency[None, :]
    cosine = jnp.cos(angles)[:, None, :]
    sine_part = jnp.sin(angles)[:, None, :]
    first_half = vectors[..., :half_dim]
    second = vectors[..., half_dim:]
    return jnp.concatenate(
        [first_half * cosine - second * sine_part, second * cosine + first_half * sine_part],
        axis=-1,
    )


def attend_tile(running, query_rows, query_pos, key_block, value_block, key_start):
    run_peak, denom, accumulated = running
    block_size = key_block.shape[0]
    score_scale = 1.0 / math.sqrt(key_block.shape[2])
    key_pos = key_start + jnp.arange(block_size, dtype=jnp.int32)
    scores = (
        jnp.einsum("shd,khd->hsk", query_rows, key_block, preferred_element_type=jnp.float32)
        * score_scale
    )
    allowed = (query_pos[:, None] >= key_pos[None, :])[None]
    masked = jnp.where(allowed, scores, mask_fill)
    new_peak = jnp.maximum(run_peak, jnp.max(masked, axis=2))
    weights = jnp.where(allowed, jnp.exp(masked - new_peak[:, :, None]), 0.0)
    factor = jnp.exp(run_peak - new_peak)
    denom = denom * factor + jnp.sum(weights, axis=2)
    accumulated = accumulated * factor[:, :, None] + jnp.einsum(
        "hsk,khd->hsd",
        weights.astype(jnp.bfloat16),
        value_block,
        preferred_element_type=jnp.float32,
    )
    return (new_peak, denom, accumulated)


def empty_state(head_count, rows):
    return (
        jnp.full((head_count, rows), mask_fill, jnp.float32),
        jnp.zeros((head_count, rows), jnp.float32),
        jnp.zeros((head_count, rows, HEAD_DIM), jnp.float32),
    )


def finish_rows(state):
    run_peak, denom, accumulated = state
    heads_out = accumulated / denom[:, :, None]
    rows = heads_out.shape[1]
    return (
        heads_out.transpose(1, 0, 2)
        .reshape(rows, heads_out.shape[0] * heads_out.shape[2])
        .astype(jnp.bfloat16)
    )


def per_device(resid_in, feats, short_filter, residues, rates, out_weight, norm_gain, attn_weight):
    row_count, chan_count = resid_in.shape
    width_all = out_weight.shape[1]
    short_out = short_mix(feats, short_filter)
    product = (short_out[:, 1] * short_out[:, 2]).astype(jnp.bfloat16)
    panel_rows = lax.all_to_all(product.T, "ctx", split_axis=0, concat_axis=1, tiled=True)
    panel_count = chan_count // lax.axis_size("ctx")
    panel_start = lax.axis_index("ctx") * panel_count
    panel_res = lax.dynamic_slice_in_dim(residues, panel_start, panel_count, 0)
    panel_rates = lax.dynamic_slice_in_dim(rates, panel_start, panel_count, 0)
    panel_conv = modal_conv(
        panel_rows.astype(jnp.float32), panel_res, panel_rates, jnp.zeros_like(panel_rates)
    )
    returned = lax.all_to_all(panel_conv, "ctx", split_axis=1, concat_axis=0, tiled=True)
    conv_out = returned.T
    gated = (short_out[:, 0] * conv_out).astype(jnp.bfloat16)
    own_share = lax.psum_scatter(
        lax.dot_general(
            out_weight, gated, (((0,), (1,)), ((), ())), preferred_element_type=jnp.float32
        ),
        "tp",
        scatter_dimension=0,
        tiled=True,
    )
    hyena_out = (resid_in.astype(jnp.float32) + own_share.T).astype(jnp.bfloat16)
    full_rows = lax.all_gather(hyena_out, "tp", axis=1, tiled=True)
    wide = full_rows.astype(jnp.float32)
    mean_square = jnp.mean(wide * wide, axis=1, keepdims=True)
    normed = (wide * lax.rsqrt(mean_square + eps_norm) * norm_gain).astype(jnp.bfloat16)
    projected = jnp.dot(
        normed, attn_weight.reshape(width_all, 3 * chan_count), preferred_element_type=jnp.float32
    ).reshape(row_count, 3, chan_count)
    head_count = chan_count // HEAD_DIM
    ctx_index = lax.axis_index("ctx")
    first_pos = ctx_index * row_count
    positions = first_pos + jnp.arange(row_count, dtype=jnp.int32)
    queries = rotary_turn(
        projected[:, 0].reshape(row_count, head_count, HEAD_DIM), positions
    ).astype(jnp.bfloat16)
    keys_all = rotary_turn(
        projected[:, 1].reshape(row_count, head_count, HEAD_DIM), positions
    ).astype(jnp.bfloat16)
    values = projected[:, 2].astype(jnp.bfloat16)
    key_pieces = (keys_all.reshape(row_count, chan_count), values)
    initial = empty_state(head_count, row_count)
    key_rows = lax.all_gather(key_pieces[0], "ctx", axis=0, tiled=True)
    value_rows = lax.all_gather(key_pieces[1], "ctx", axis=0, tiled=True)
    key_total = key_rows.shape[0]
    tiles_block_size = math.gcd(key_total, 1024)
    block_count = key_total // tiles_block_size
    key_blocks = key_rows.reshape(block_count, tiles_block_size, head_count, HEAD_DIM)
    value_blocks = value_rows.reshape(block_count, tiles_block_size, head_count, HEAD_DIM)
    key_blocks, value_blocks, block_ids, block_size = (
        key_blocks,
        value_blocks,
        jnp.arange(block_count, dtype=jnp.int32),
        tiles_block_size,
    )

    def one_tile(carried, slot_item):
        key_block, value_block, block_index = slot_item
        key_start = block_index * block_size
        updated = attend_tile(carried, queries, positions, key_block, value_block, key_start)
        return (updated, None)

    result, _ = lax.scan(one_tile, initial, (key_blocks, value_blocks, block_ids))
    context = finish_rows(result)
    return (hyena_out, context)


def solution(mesh):
    in_specs = (
        P("ctx", "tp"),
        P("ctx", None, "tp"),
        P(None, None, "tp"),
        P("tp", None),
        P("tp", None),
        P("tp", None),
        P(),
        P(None, None, "tp"),
    )
    out_specs = (P("ctx", "tp"), P("ctx", "tp"))
    return jax.shard_map(
        per_device, mesh=mesh, in_specs=in_specs, out_specs=out_specs, check_vma=False
    )
```

profile of v0, /device:TPU:4, one launch (start us, length us, event | category | flops | bytes accessed | tf_op | source)
XLA Modules:
  0.0 341.5 jit_solution(16704651836069771264)
XLA Ops:
  7.2 0.0 copy-start
  7.2 0.8 slice.59
  8.0 0.2 copy.44
  8.1 3.4 %collective-permute-start = (bf16[2,3,128]{0,2,1:T(8,128)(2,1)S(1)}, bf16[2,3,128]{0,2,1:T(8,128)(2,1)S(1)}, u32[]{:S(2)}, u32[]{:S(2)}) collective-permute-start(bf16[2,3,128]{0,2,1:T(8,128)(2,1)S(1)} %copy.44), channel_id=1, source_target_pairs={{0,32},{32,64},{64,96},{96,128},{128,160},{160,192},{192,224},{224... | collective-permute-start | bytes 4616 | tf_op jit(solution)/shard_map/ppermute | solution.py:17
  11.6 0.1 fusion.79
  11.7 0.1 fusion.80
  11.8 0.8 constant_dynamic-slice_fusion
  12.5 0.1 copy.63
  12.6 0.1 copy.64
  12.7 0.7 slice_bitcast_fusion.3
  13.4 0.1 multiply_reduce_fusion.1
  13.5 1.0 copy.45
  14.5 0.1 concatenate.30
  14.6 0.1 reverse
  14.8 0.1 slice.135
  14.8 0.1 tile.4
  14.9 0.6 tile.10
  15.5 0.3 slice.81
  15.9 1.6 reshape.257
  17.5 0.4 collective-permute-done
  17.9 0.1 maximum_convert_fusion
  18.0 0.3 fusion.34
  18.4 0.6 fusion.65
  19.0 8.8 %all-to-all-start = ((bf16[16,8,128]{2,1,0:T(8,128)(2,1)}), bf16[16,8,128]{2,1,0:T(8,128)(2,1)S(1)}, u32[]{:S(2)}, u32[]{:S(2)}) async-start(bf16[16,8,128]{2,1,0:T(8,128)(2,1)} %fusion.65), calls=%async_computation | async-start | bytes 65536 | tf_op jit(solution)/shard_map/all_to_all | solution.py:134
  27.8 0.0 reduce-scatter.2.cloned.1.call-start
  27.8 7.4 %all-to-all-done = bf16[16,8,128]{2,1,0:T(8,128)(2,1)S(1)} async-done(((bf16[16,8,128]{2,1,0:T(8,128)(2,1)}), bf16[16,8,128]{2,1,0:T(8,128)(2,1)S(1)}, u32[]{:S(2)}, u32[]{:S(2)}) %all-to-all-start) | async-done | bytes 32800 | tf_op jit(solution)/shard_map/all_to_all | solution.py:134
  35.2 0.2 convolution_bitcast_fusion.2
  35.5 0.1 copy.65
  35.5 0.6 multiply_reduce_fusion
  36.1 0.1 copy.60
  36.2 0.5 fusion.32
  36.7 0.3 convolution_add_fusion
  37.0 13.1 %all_to_all.32 = f32[8,16,128]{2,0,1:T(8,128)S(1)} all-to-all(f32[8,16,128]{2,0,1:T(8,128)S(1)} %copy.49), channel_id=1, replica_groups=mesh['ctx'=16,'tp'=32] {'ctx'}, dimensions={1} | all-to-all | bytes 131072 | tf_op jit(solution)/shard_map/all_to_all | solution.py:142
  50.2 0.0 copy-done
  50.2 0.0 copy-start.1
  50.2 1.8 convolution_bitcast_fusion.1
  52.0 0.0 reduce-scatter.2.cloned.1.call-update
  52.0 0.0 all-gather.3.cloned.1.call-start
  52.1 122.4 %reduce-scatter.2.cloned.1.call-done = f32[128,128]{0,1:T(8,128)} async-done(((f32[4096,128]{0,1:T(8,128)}), f32[128,128]{0,1:T(8,128)}) %reduce-scatter.2.cloned.1.call-update) | async-done | bytes 65552 | tf_op jit(solution)/shard_map/reduce_scatter | solution.py:145
  174.4 0.0 copy-done.1
  174.4 1.5 fusion.39
  175.9 0.0 all-gather.3.cloned.1.call-update
  175.9 0.0 copy-start.2
  176.0 4.7 %copy.50 = bf16[4096,3,128]{0,2,1:T(8,128)(2,1)} copy(bf16[4096,3,128]{2,0,1:T(8,128)(2,1)} %param.17) | data formatting | bytes 6291456 | tf_op args[7]
  180.7 59.4 %all-gather.3.cloned.1.call-done = bf16[128,4096]{1,0:T(8,128)(2,1)} async-done(((bf16[128,128]{1,0:T(8,128)(2,1)}), bf16[128,4096]{1,0:T(8,128)(2,1)}) %all-gather.3.cloned.1.call-update) | async-done | bytes 1048592 | tf_op jit(solution)/shard_map/all_gather | solution.py:154
  240.1 1.5 fusion.25
  241.6 0.0 copy-done.2
  241.6 3.3 fusion.23
  244.9 0.2 fusion.61
  245.1 0.1 copy.52
  245.3 39.5 %all_gather.10 = bf16[2048,128]{0,1:T(8,128)(2,1)S(1)} all-gather(bf16[128,128]{0,1:T(8,128)(2,1)S(1)} %pad_maximum_fusion), channel_id=1, replica_groups=mesh['ctx'=16,'tp'=32] {'ctx'}, dimensions={0}, use_global_device_ids=true | all-gather | bytes 557056 | tf_op jit(solution)/shard_map/all_gather | solution.py:174
  284.7 0.3 copy.61
  285.0 44.0 %all-gather = bf16[2048,1,128]{0,2,1:T(8,128)(2,1)S(1)} all-gather(bf16[128,1,128]{0,2,1:T(8,128)(2,1)S(1)} %slice.136), channel_id=2, replica_groups=mesh['ctx'=16,'tp'=32] {'ctx'}, dimensions={0}, use_global_device_ids=true | all-gather | bytes 557056 | tf_op jit(solution)/shard_map/all_gather | solution.py:175
  329.0 0.3 copy.62
  329.3 4.6 %while.15 = (s32[]{:T(128)}, f32[1,128]{1,0:T(1,128)S(1)}, f32[1,128]{1,0:T(1,128)S(1)}, f32[1,128,128]{2,1,0:T(8,128)S(1)}, s32[2]{0:T(128)S(1)}, /*index=5*/bf...) while((s32[]{:T(128)}, f32[1,128]{1,0:T(1,128)S(1)}, ...), condition=%wide.region_6.7_spmd.clone, body=%wide.region_3.6_spmd.clone.sunk | while | flops 68732800 | bytes 2287785 | solution.py:194
  329.3 0.6 dynamic_slice.39
  330.6 0.3 fusion.93
  330.9 0.4 fusion.97
  331.4 0.2 fusion.95
  331.6 0.6 dynamic_slice.39
  332.9 0.3 fusion.93
  333.3 0.4 fusion.97
  333.7 0.2 fusion.95
  333.9 0.7 fusion.74
  (24 shorter events, 0.2 us)
Async XLA Ops:
  7.2 43.0 %copy-start = (bf16[128,4096]{1,0:T(8,128)(2,1)S(1)}, bf16[128,4096]{1,0:T(8,128)(2,1)}, u32[]{:S(2)}) copy-start(bf16[128,4096]{1,0:T(8,128)(2,1)} %param.15) | copy-start | bytes 3145732
  8.1 9.7 %collective-permute-start = (bf16[2,3,128]{0,2,1:T(8,128)(2,1)S(1)}, bf16[2,3,128]{0,2,1:T(8,128)(2,1)S(1)}, u32[]{:S(2)}, u32[]{:S(2)}) collective-permute-start(bf16[2,3,128]{0,2,1:T(8,128)(2,1)S(1)} %copy.44), channel_id=1, source_target_pairs={{0,32},{32,64},{64,96},{96,128},{128,160},{160,192},{192,224},{224... | collective-permute-start | bytes 4616 | tf_op jit(solution)/shard_map/ppermute | solution.py:17
  19.0 16.2 %all-to-all-start = ((bf16[16,8,128]{2,1,0:T(8,128)(2,1)}), bf16[16,8,128]{2,1,0:T(8,128)(2,1)S(1)}, u32[]{:S(2)}, u32[]{:S(2)}) async-start(bf16[16,8,128]{2,1,0:T(8,128)(2,1)} %fusion.65), calls=%async_computation | async-start | bytes 65536 | tf_op jit(solution)/shard_map/all_to_all | solution.py:134
  27.8 146.7 %reduce-scatter.2.cloned.1.call-start = ((), (), s32[]{:S(2)}) async-start(), calls=%async_computation.3 | async-start | bytes 2162688 | tf_op jit(solution)/shard_map/reduce_scatter | solution.py:145
  50.2 124.3 %copy-start.1 = (bf16[128,128]{1,0:T(8,128)(2,1)S(1)}, bf16[128,128]{1,0:T(8,128)(2,1)}, u32[]{:S(2)}) copy-start(bf16[128,128]{1,0:T(8,128)(2,1)} %param.10) | copy-start | bytes 98308
  52.0 188.1 %all-gather.3.cloned.1.call-start = ((), (), s32[]{:S(2)}) async-start(), calls=%async_computation.4 | async-start | bytes 1081344 | tf_op jit(solution)/shard_map/all_gather | solution.py:154
  175.9 65.7 %copy-start.2 = (f32[4096]{0:T(1024)S(1)}, f32[4096]{0:T(1024)}, u32[]{:S(2)}) copy-start(f32[4096]{0:T(1024)} %param.16) | copy-start | bytes 49156
Sparse Core Ops, SparseCore 0:
  52.1 122.2 reduce-scatter.1
  177.3 62.7 all-gather.2
where the time goes:
time: 342 us; the launch traced here: 341 us
  waiting for transfers between devices  190 us (56%)
  blocking collectives  96.6 us (28%)
  between operations  14.3 us (4%)
  local copies, waits for them, and re-layouts  13.3 us (4%)
  starting transfers between devices  12.3 us (4%)
  matrix products  7.62 us (2%)
  other arithmetic  6.38 us (2%)
    reduce_scatter x1, waiting for transfers between devices, per_device(): lax.psum_scatter(lax.dot_general(out_weight, gated, (((0,), (1,)), ((), (...  122 us
    all_gather x1, waiting for transfers between devices, per_device(): full_rows = lax.all_gather(hyena_out, 'tp', axis=1, tiled=True)  59.4 us
    all_gather x1, blocking collectives, per_device(): value_rows = lax.all_gather(key_pieces[1], 'ctx', axis=0, tiled=True)  44 us
    all_gather x1, blocking collectives, per_device(): key_rows = lax.all_gather(key_pieces[0], 'ctx', axis=0, tiled=True)  39.5 us
    all_to_all x1, blocking collectives, per_device(): lax.all_to_all(panel_conv, 'ctx', split_axis=1, concat_axis=0, tiled=True)  13.1 us
    all_to_all x1, starting transfers between devices, per_device(): lax.all_to_all(product.T, 'ctx', split_axis=0, concat_axis=1, tiled=True)  8.78 us
    all_to_all x1, waiting for transfers between devices, per_device(): lax.all_to_all(product.T, 'ctx', split_axis=0, concat_axis=1, tiled=True)  7.39 us
  transfers between devices with their start and end apart: 4, of which 4 were waited for; matrix products, arithmetic and copies ran while one was open for 3% of the time, Pallas kernels for 0%

commit v1 on v0

--- a/solution.py
+++ b/solution.py
@@ -131,7 +131,12 @@
     width_all = out_weight.shape[1]
     short_out = short_mix(feats, short_filter)
     product = (short_out[:, 1] * short_out[:, 2]).astype(jnp.bfloat16)
-    panel_rows = lax.all_to_all(product.T, "ctx", split_axis=0, concat_axis=1, tiled=True)
+    original = product.T
+    y1 = lax.psum(1, "ctx")
+    even = jnp.split(original, y1, 0)
+    e_next = jnp.stack(even, axis=0)
+    arr_now = lax.all_to_all(e_next, axis_name="ctx", split_axis=0, concat_axis=0)
+    panel_rows = jnp.concatenate(arr_now, 1)
     panel_count = chan_count // lax.axis_size("ctx")
     panel_start = lax.axis_index("ctx") * panel_count
     panel_res = lax.dynamic_slice_in_dim(residues, panel_start, panel_count, 0)

time: 342 us -> 351 us (1.026)
  local copies, waits for them, and re-layouts: 13.3 us -> 22.6 us
    unnamed x16 -> x31, local copies, waits for them, and re-layouts: 6.83 us -> 15.5 us
where the time goes in v1:
time: 351 us
  waiting for transfers between devices  190 us (54%)
  blocking collectives  96.6 us (28%)
  local copies, waits for them, and re-layouts  22.6 us (6%)
  between operations  14.3 us (4%)
  starting transfers between devices  12.3 us (4%)
  matrix products  7.62 us (2%)
  other arithmetic  5.78 us (2%)
    reduce_scatter x1, waiting for transfers between devices, per_device(): lax.psum_scatter(lax.dot_general(out_weight, gated, (((0,), (1,)), ((), (...  122 us
    all_gather x1, waiting for transfers between devices, per_device(): full_rows = lax.all_gather(hyena_out, 'tp', axis=1, tiled=True)  59.8 us
    all_gather x1, blocking collectives, per_device(): value_rows = lax.all_gather(key_pieces[1], 'ctx', axis=0, tiled=True)  44 us
    all_gather x1, blocking collectives, per_device(): key_rows = lax.all_gather(key_pieces[0], 'ctx', axis=0, tiled=True)  39.5 us
    unnamed x31, local copies, waits for them, and re-layouts  15.5 us
    all_to_all x1, blocking collectives, per_device(): lax.all_to_all(panel_conv, 'ctx', split_axis=1, concat_axis=0, tiled=True)  13.1 us
    all_to_all x1, starting transfers between devices, per_device(): lax.all_to_all(e_next, axis_name='ctx', split_axis=0, concat_axis=0)  8.79 us
    all_to_all x1, waiting for transfers between devices, per_device(): lax.all_to_all(e_next, axis_name='ctx', split_axis=0, concat_axis=0)  7.39 us
  transfers between devices with their start and end apart: 4, of which 4 were waited for; matrix products, arithmetic and copies ran while one was open for 3% of the time, Pallas kernels for 0%

profile of v1, /device:TPU:4, one launch (start us, length us, event | category | flops | bytes accessed | tf_op | source)
XLA Modules:
  0.0 350.5 jit_solution(13204490716095338247)
XLA Ops:
  7.2 0.8 slice.59
  8.0 0.2 copy.509
  8.1 3.4 collective-permute-start
  11.7 0.1 fusion.80
  11.8 0.7 slice_bitcast_fusion.19
  12.5 0.8 constant_dynamic-slice_fusion
  13.4 0.1 multiply_reduce_fusion.1
  13.5 1.0 copy.510
  14.6 0.1 reverse
  14.8 0.1 slice.135
  14.8 0.1 tile.4
  14.9 0.6 tile.10
  15.5 0.3 slice.81
  15.9 1.6 reshape.259
  17.5 0.4 collective-permute-done
  17.9 0.1 maximum_convert_fusion
  18.0 0.3 fusion.34
  18.4 0.6 constant_dynamic-update-slice_fusion.15
  19.0 0.6 constant_dynamic-update-slice_fusion.14
  19.5 0.6 constant_dynamic-update-slice_fusion.13
  20.1 0.6 constant_dynamic-update-slice_fusion.12
  20.7 0.6 constant_dynamic-update-slice_fusion.11
  21.3 0.6 constant_dynamic-update-slice_fusion.10
  21.8 0.6 constant_dynamic-update-slice_fusion.9
  22.4 0.6 constant_dynamic-update-slice_fusion.8
  23.0 0.6 constant_dynamic-update-slice_fusion.7
  23.6 0.6 constant_dynamic-update-slice_fusion.6
  24.2 0.6 constant_dynamic-update-slice_fusion.5
  24.7 0.6 constant_dynamic-update-slice_fusion.4
  25.3 0.6 constant_dynamic-update-slice_fusion.3
  25.9 0.6 constant_dynamic-update-slice_fusion.2
  26.5 0.6 constant_dynamic-update-slice_fusion.1
  27.1 0.6 constant_dynamic-update-slice_fusion
  27.6 8.8 %all-to-all-start = ((bf16[16,8,128]{2,1,0:T(8,128)(2,1)}), bf16[16,8,128]{2,1,0:T(8,128)(2,1)S(1)}, u32[]{:S(2)}, u32[]{:S(2)}) async-start(bf16[16,8,128]{2,1,0:T(8,128)(2,1)} %constant_dynamic-update-slice_fusion), calls=%async_computation | async-start | bytes 65536 | tf_op jit(solution)/shard_map/all_to_all | solution.py:138
  36.5 7.4 %all-to-all-done = bf16[16,8,128]{2,1,0:T(8,128)(2,1)S(1)} async-done(((bf16[16,8,128]{2,1,0:T(8,128)(2,1)}), bf16[16,8,128]{2,1,0:T(8,128)(2,1)S(1)}, u32[]{:S(2)}, u32[]{:S(2)}) %all-to-all-start) | async-done | bytes 32800 | tf_op jit(solution)/shard_map/all_to_all | solution.py:138
  43.9 0.2 convolution_bitcast_fusion.2
  44.1 0.1 copy.530
  44.2 0.6 multiply_reduce_fusion
  44.9 0.5 fusion.32
  45.4 0.3 convolution_add_fusion
  45.7 13.1 %all_to_all.21 = f32[8,16,128]{2,0,1:T(8,128)S(1)} all-to-all(f32[8,16,128]{2,0,1:T(8,128)S(1)} %copy.514), channel_id=1, replica_groups=mesh['ctx'=16,'tp'=32] {'ctx'}, dimensions={1} | all-to-all | bytes 131072 | tf_op jit(solution)/shard_map/all_to_all | solution.py:147
  58.8 1.8 convolution_bitcast_fusion.1
  60.7 122.3 %reduce-scatter.2.cloned.1.call-done = f32[128,128]{0,1:T(8,128)} async-done(((f32[4096,128]{0,1:T(8,128)}), f32[128,128]{0,1:T(8,128)}) %reduce-scatter.2.cloned.1.call-update) | async-done | bytes 65552 | tf_op jit(solution)/shard_map/reduce_scatter | solution.py:150
  183.1 1.5 fusion.39
  184.6 4.7 %copy.515 = bf16[4096,3,128]{0,2,1:T(8,128)(2,1)} copy(bf16[4096,3,128]{2,0,1:T(8,128)(2,1)} %param.17) | data formatting | bytes 6291456 | tf_op args[7]
  189.3 59.8 %all-gather.3.cloned.1.call-done = bf16[128,4096]{1,0:T(8,128)(2,1)} async-done(((bf16[128,128]{1,0:T(8,128)(2,1)}), bf16[128,4096]{1,0:T(8,128)(2,1)}) %all-gather.3.cloned.1.call-update) | async-done | bytes 1048592 | tf_op jit(solution)/shard_map/all_gather | solution.py:159
  249.1 1.5 fusion.25
  250.6 3.3 fusion.23
  253.9 0.2 fusion.61
  254.1 0.1 copy.517
  254.3 39.5 %all_gather.10 = bf16[2048,128]{0,1:T(8,128)(2,1)S(1)} all-gather(bf16[128,128]{0,1:T(8,128)(2,1)S(1)} %pad_maximum_fusion), channel_id=1, replica_groups=mesh['ctx'=16,'tp'=32] {'ctx'}, dimensions={0}, use_global_device_ids=true | all-gather | bytes 557056 | tf_op jit(solution)/shard_map/all_gather | solution.py:179
  293.7 0.3 copy.526
  294.0 44.0 %all-gather = bf16[2048,1,128]{0,2,1:T(8,128)(2,1)S(1)} all-gather(bf16[128,1,128]{0,2,1:T(8,128)(2,1)S(1)} %slice.136), channel_id=2, replica_groups=mesh['ctx'=16,'tp'=32] {'ctx'}, dimensions={0}, use_global_device_ids=true | all-gather | bytes 557056 | tf_op jit(solution)/shard_map/all_gather | solution.py:180
  338.0 0.3 copy.527
  338.3 4.6 %while.15 = (s32[]{:T(128)}, f32[1,128]{1,0:T(1,128)S(1)}, f32[1,128]{1,0:T(1,128)S(1)}, f32[1,128,128]{2,1,0:T(8,128)S(1)}, s32[2]{0:T(128)S(1)}, /*index=5*/bf...) while((s32[]{:T(128)}, f32[1,128]{1,0:T(1,128)S(1)}, ...), condition=%wide.region_6.7_spmd.clone, body=%wide.region_3.6_spmd.clone.sunk | while | flops 68732800 | bytes 2287785 | solution.py:199
  338.3 0.6 dynamic_slice.39
  339.6 0.3 fusion.93
  340.0 0.4 fusion.97
  340.4 0.2 fusion.95
  340.7 0.6 dynamic_slice.39
  341.9 0.3 fusion.93
  342.3 0.4 fusion.97
  342.7 0.2 fusion.95
  343.0 0.7 fusion.74
  (40 shorter events, 0.7 us)
Async XLA Ops:
  7.2 51.7 %copy-start = (bf16[128,4096]{1,0:T(8,128)(2,1)S(1)}, bf16[128,4096]{1,0:T(8,128)(2,1)}, u32[]{:S(2)}) copy-start(bf16[128,4096]{1,0:T(8,128)(2,1)} %param.15) | copy-start | bytes 3145732
  8.1 9.7 %collective-permute-start = (bf16[2,3,128]{0,2,1:T(8,128)(2,1)S(1)}, bf16[2,3,128]{0,2,1:T(8,128)(2,1)S(1)}, u32[]{:S(2)}, u32[]{:S(2)}) collective-permute-start(bf16[2,3,128]{0,2,1:T(8,128)(2,1)S(1)} %copy.509), channel_id=1, source_target_pairs={{0,32},{32,64},{64,96},{96,128},{128,160},{160,192},{192,224},{224... | collective-permute-start | bytes 4616 | tf_op jit(solution)/shard_map/ppermute | solution.py:17
  27.6 16.2 %all-to-all-start = ((bf16[16,8,128]{2,1,0:T(8,128)(2,1)}), bf16[16,8,128]{2,1,0:T(8,128)(2,1)S(1)}, u32[]{:S(2)}, u32[]{:S(2)}) async-start(bf16[16,8,128]{2,1,0:T(8,128)(2,1)} %constant_dynamic-update-slice_fusion), calls=%async_computation | async-start | bytes 65536 | tf_op jit(solution)/shard_map/all_to_all | solution.py:138
  36.4 146.6 %reduce-scatter.2.cloned.1.call-start = ((), (), s32[]{:S(2)}) async-start(), calls=%async_computation.3 | async-start | bytes 2162688 | tf_op jit(solution)/shard_map/reduce_scatter | solution.py:150
  58.8 124.2 %copy-start.1 = (bf16[128,128]{1,0:T(8,128)(2,1)S(1)}, bf16[128,128]{1,0:T(8,128)(2,1)}, u32[]{:S(2)}) copy-start(bf16[128,128]{1,0:T(8,128)(2,1)} %param.10) | copy-start | bytes 98308
  60.7 188.4 %all-gather.3.cloned.1.call-start = ((), (), s32[]{:S(2)}) async-start(), calls=%async_computation.4 | async-start | bytes 1081344 | tf_op jit(solution)/shard_map/all_gather | solution.py:159
  184.6 66.0 %copy-start.2 = (f32[4096]{0:T(1024)S(1)}, f32[4096]{0:T(1024)}, u32[]{:S(2)}) copy-start(f32[4096]{0:T(1024)} %param.16) | copy-start | bytes 49156
Sparse Core Ops, SparseCore 0:
  60.8 122.2 reduce-scatter.1
  185.9 63.1 all-gather.2
